TPU v7x, 32 devices: a whole 2x2x4 slice. The times are simulated.
32 devices in a mesh: groups: 2 (over x), seq: 4 (over y, core), pair: 4 (over z).
Axes of the slice: x: 2, y: 2, z: 4, core: 2. Of those that a mesh axis runs over, the one named last changes fastest.
Arguments:
- sequence: bfloat16 [4096, 1536], P(('groups', 'seq', 'pair')), parts along dimension 0, may hold values from -12 to 12
- gain_conv: float32 [1536], replicated, may hold values from 0.25 to 1.75
- conv_weight: bfloat16 [5, 1536, 1536], P(None, 'pair'), may hold values from -0.0625 to 0.0625
- gain_attn: float32 [1536], replicated, may hold values from 0.25 to 1.75
- w_qkv: bfloat16 [1536, 3072], P(None, 'pair'), may hold values from -1 to 1
- w_out: bfloat16 [1024, 1536], P('pair'), may hold values from -0.75 to 0.75
- gain_pool: float32 [1536], replicated, may hold values from 0.25 to 1.75
- w_pair: bfloat16 [1536, 256], replicated, may hold values from -0.15625 to 0.15625
- w_up: bfloat16 [128, 256], replicated, may hold values from -0.5 to 0.5
- w_down: bfloat16 [256, 128], replicated, may hold values from -0.375 to 0.375
Outputs:
- seq_out: bfloat16 [4096, 1536], P(('groups', 'seq', 'pair')), parts along dimension 0
- pair_map: bfloat16 [256, 128, 128], P(('groups', 'seq'), 'pair'), parts along dimension 0
There are 2 independent parts, one for each index of `groups`. A program takes and returns all parts, laid end to end along the dimension named above; an argument that names none is the same for every part. Nothing has to cross between parts.
All inputs are finite; a program needn't handle non-finite values.
Results may differ from a plain program's by a relative error of at most 0.024.
Values may be sent and summed in bfloat16 or wider, within the bound.
No kernel may reach another device: no remote copies, remote signals or barrier semaphores. Data moves between devices by JAX's collectives and lax.ppermute only.
A program may use at most 64 MiB of HBM per device.

v0:
```python
import math
import jax
import jax.numpy as jnp
from jax import lax
from jax.sharding import PartitionSpec as P

KEY_SIZE = 128
VALUE_SIZE = 128
DILATION = 4
POOL = 16
PAIR_CH = 128
EPS = 1e-06


def padded_2(value, sides, width):
    for axis, dim in sides:
        peers, length = (lax.axis_size(axis), value.shape[dim])
        up = [(i, (i + 1) % peers) for i in range(peers - 1)]
        down = [(j, i) for i, j in up]
        last = lax.slice_in_dim(value, length - width, length, axis=dim)
        first = lax.slice_in_dim(value, 0, width, axis=dim)
        before = lax.ppermute(last, axis, up)
        after = lax.ppermute(first, axis, down)
        value = jnp.concatenate([before, value, after], axis=dim)
    return value


def norm_rows(values, gain):
    return values * lax.rsqrt(jnp.mean(values * values, axis=-1, keepdims=True) + EPS) * gain


def conv_rows(padded, conv_weight, row_total):
    summed = jnp.zeros((row_total, conv_weight.shape[2]), jnp.float32)
    for offset in range(conv_weight.shape[0]):
        shifted = lax.dynamic_slice_in_dim(padded, offset * DILATION, row_total, 0)
        summed = summed + jnp.dot(shifted, conv_weight[offset], preferred_element_type=jnp.float32)
    return summed


def shards(
    sequence, gain_conv, conv_weight, gain_attn, w_qkv, w_out, gain_pool, w_pair, w_up, w_down
):
    pair_count = lax.axis_size("pair")
    seq_count = lax.axis_size("seq")
    row_count = sequence.shape[0]
    channels = sequence.shape[1]
    local_rows = row_count * pair_count
    inputs = sequence.astype(jnp.float32)
    normed = norm_rows(inputs, gain_conv).astype(jnp.bfloat16)
    swapped = lax.all_to_all(normed, "pair", split_axis=1, concat_axis=0, tiled=True)
    padded = padded_2(swapped, (("seq", 0),), DILATION * (conv_weight.shape[0] - 1) // 2)
    summed = lax.psum_scatter(
        conv_rows(padded, conv_weight, row_count * lax.axis_size("pair")),
        "pair",
        scatter_dimension=0,
        tiled=True,
    )
    first_out = (inputs + summed).astype(jnp.bfloat16)
    attn_in = norm_rows(first_out.astype(jnp.float32), gain_attn).astype(jnp.bfloat16)
    projected = jnp.dot(
        lax.all_gather(attn_in, "pair", axis=0, tiled=True),
        w_qkv,
        preferred_element_type=jnp.float32,
    ).astype(jnp.bfloat16)
    head_count = projected.shape[1] // (2 * KEY_SIZE + VALUE_SIZE)
    grouped = projected.reshape(local_rows, head_count, 2 * KEY_SIZE + VALUE_SIZE)
    queries = grouped[:, :, :KEY_SIZE]
    key_rows = grouped[:, :, KEY_SIZE : 2 * KEY_SIZE].reshape(local_rows, head_count * KEY_SIZE)
    value_rows = grouped[:, :, 2 * KEY_SIZE :].reshape(local_rows, head_count * VALUE_SIZE)
    scale = 1.0 / math.sqrt(KEY_SIZE)
    start_state = (
        jnp.full((head_count, local_rows), -1e30, jnp.float32),
        jnp.zeros((head_count, local_rows), jnp.float32),
        jnp.zeros((head_count, local_rows, VALUE_SIZE), jnp.float32),
    )
    carried = start_state
    key_piece = lax.all_gather(key_rows, "seq", axis=0, tiled=True)
    value_piece = lax.all_gather(value_rows, "seq", axis=0, tiled=True)
    piece_rows = key_piece.shape[0]
    block_rows = math.gcd(piece_rows, 512)
    block_count = piece_rows // block_rows
    key_blocks = key_piece.reshape(block_count, block_rows, head_count, KEY_SIZE)
    value_blocks = value_piece.reshape(block_count, block_rows, head_count, VALUE_SIZE)

    def one_block(state, blocks):
        running_max, running_sum, weighted = state
        key_block, value_block = blocks
        scores = (
            jnp.einsum("qhd,khd->hqk", queries, key_block, preferred_element_type=jnp.float32)
            * scale
        )
        new_max = jnp.maximum(running_max, jnp.max(scores, axis=-1))
        shrink = jnp.exp(running_max - new_max)
        weights = jnp.exp(scores - new_max[:, :, None])
        running_sum = running_sum * shrink + jnp.sum(weights, axis=-1)
        update = jnp.einsum(
            "hqk,khd->hqd",
            weights.astype(jnp.bfloat16),
            value_block,
            preferred_element_type=jnp.float32,
        )
        weighted = weighted * shrink[:, :, None] + update
        return ((new_max, running_sum, weighted), None)

    carried, unused = lax.scan(one_block, carried, (key_blocks, value_blocks))
    running_max, running_sum, weighted = carried
    attended = (weighted / running_sum[:, :, None]).astype(jnp.bfloat16)
    attended = attended.transpose(1, 0, 2).reshape(local_rows, head_count * VALUE_SIZE)
    mixed = lax.psum_scatter(
        jnp.dot(attended, w_out, preferred_element_type=jnp.float32).astype(jnp.bfloat16),
        "pair",
        scatter_dimension=0,
        tiled=True,
    ).astype(jnp.float32)
    seq_out = (first_out.astype(jnp.float32) + mixed).astype(jnp.bfloat16)
    bin_count = row_count // POOL
    pooled = jnp.mean(seq_out.astype(jnp.float32).reshape(bin_count, POOL, channels), axis=1)
    bin_norm = norm_rows(pooled, gain_pool).astype(jnp.bfloat16)
    sides = jnp.dot(bin_norm, w_pair, preferred_element_type=jnp.float32).astype(jnp.bfloat16)
    left_side = sides[:, :PAIR_CH]
    right_side = sides[:, PAIR_CH:]
    tile_rows = bin_count * pair_count
    tile_cols = bin_count * seq_count
    row_side = lax.all_gather(left_side, "pair", axis=0, tiled=True)
    all_right = lax.all_gather(right_side, ("seq", "pair"), axis=0, tiled=True)
    column_side = lax.dynamic_slice_in_dim(
        all_right, lax.axis_index("pair") * tile_cols, tile_cols, 0
    )
    pair_tile = (
        row_side.astype(jnp.float32)[:, None, :] * column_side.astype(jnp.float32)[None, :, :]
    ).astype(jnp.bfloat16)
    flat_rows = pair_tile.reshape(tile_rows * tile_cols, PAIR_CH)
    hidden = jax.nn.relu(jnp.dot(flat_rows, w_up, preferred_element_type=jnp.float32)).astype(
        jnp.bfloat16
    )
    pair_out = flat_rows.astype(jnp.float32) + jnp.dot(
        hidden, w_down, preferred_element_type=jnp.float32
    )
    pair_map = pair_out.astype(jnp.bfloat16).reshape(tile_rows, tile_cols, PAIR_CH)
    return (seq_out, pair_map)


def solution(mesh):
    return jax.shard_map(
        shards,
        mesh=mesh,
        in_specs=(
            P(("groups", "seq", "pair"), None),
            P(),
            P(None, "pair", None),
            P(),
            P(None, "pair"),
            P("pair", None),
            P(),
            P(),
            P(),
            P(),
        ),
        out_specs=(P(("groups", "seq", "pair"), None), P(("groups", "seq"), "pair", None)),
        check_vma=False,
    )
```

profile of v0, /device:TPU:0, one launch (start us, length us, event | category | flops | bytes accessed | tf_op | source)
XLA Modules:
  0.0 302.2 jit_solution(12201782446949053224)
XLA Ops:
  9.8 17.8 %all_to_all.19 = bf16[128,4,384]{2,0,1:T(8,128)(2,1)S(1)} all-to-all(bf16[128,4,384]{2,0,1:T(8,128)(2,1)S(1)} %bitcast.84), channel_id=1, replica_groups=mesh['groups'=2,'seq'=4,'pair'=4] {'pair'}, dimensions={1} | all-to-all | bytes 786432 | tf_op jit(solution)/shard_map/all_to_all | solution.py:50
  27.6 1.5 collective-permute-start
  29.1 2.4 fusion.19
  33.8 2.4 collective-permute-done.1
  38.1 2.6 fusion.10
  40.8 60.6 %reduce-scatter.3.cloned.1.call-done = f32[128,1536]{1,0:T(8,128)} async-done(((f32[512,1536]{1,0:T(8,128)}), f32[128,1536]{1,0:T(8,128)}) %reduce-scatter.3.cloned.1.call-update) | async-done | bytes 786448 | tf_op jit(solution)/shard_map/reduce_scatter | solution.py:52
  104.5 37.2 %all-gather.4.cloned.1.call-done = bf16[512,1536]{1,0:T(8,128)(2,1)} async-done(((bf16[128,1536]{1,0:T(8,128)(2,1)}), bf16[512,1536]{1,0:T(8,128)(2,1)}) %all-gather.4.cloned.1.call-update) | async-done | bytes 1572880 | tf_op jit(solution)/shard_map/all_gather | solution.py:61
  141.7 3.7 %convolution_convert_fusion.1 = bf16[512,768]{1,0:T(8,128)(2,1)} fusion(bf16[512,1536]{1,0:T(8,128)(2,1)} %all-gather.4.cloned.1.call-done, bf16[1536,768]{1,0:T(8,128)(2,1)S(1)} %copy-done), kind=kOutput, calls=%fused_computation.25 | convolution fusion | flops 1208352768 | bytes 4718592 | tf_op jit(solution)/shard_map/dot_general | solution.py:60
  145.4 2.1 reshape.71
  149.5 1.7 copy.43
  151.3 13.8 %all-gather.6.cloned.1.call-done = bf16[2048,256]{1,0:T(8,128)(2,1)} async-done(((bf16[512,256]{1,0:T(8,128)(2,1)}), bf16[2048,256]{1,0:T(8,128)(2,1)}) %all-gather.6.cloned.1.call-update) | async-done | bytes 1048592 | tf_op jit(solution)/shard_map/all_gather | solution.py:77
  165.2 2.2 reshape.73
  167.3 16.0 %all-gather.8.cloned.1.call-done = bf16[2048,256]{1,0:T(8,128)(2,1)} async-done(((bf16[512,256]{1,0:T(8,128)(2,1)}), bf16[2048,256]{1,0:T(8,128)(2,1)}) %all-gather.8.cloned.1.call-update) | async-done | bytes 1048592 | tf_op jit(solution)/shard_map/all_gather | solution.py:78
  183.3 2.2 reshape.75
  185.5 24.8 %while.15 = (s32[]{:T(128)}, f32[2,512]{1,0:T(2,128)S(1)}, f32[2,512]{1,0:T(2,128)S(1)}, f32[2,512,128]{2,1,0:T(8,128)S(1)}, bf16[4,512,2,128]{3,2,1,0:T(2,128)(...) while((s32[]{:T(128)}, f32[2,512]{1,0:T(2,128)S(1)}, ...), condition=%wide.region_6.7_spmd.clone, body=%wide.region_3.6_spmd.clone.sunk | while | flops 273028096 | bytes 17629320 | solution.py:105
  186.9 1.8 bitcast_reduce_fusion.2
  188.7 2.1 fusion.74
  191.7 1.4 constant_dynamic-slice_fusion.3
  193.1 1.8 bitcast_reduce_fusion.2
  194.9 2.1 fusion.74
  197.9 1.4 constant_dynamic-slice_fusion.3
  199.3 1.8 bitcast_reduce_fusion.2
  201.1 2.1 fusion.74
  204.1 1.4 constant_dynamic-slice_fusion.3
  205.5 1.8 bitcast_reduce_fusion.2
  207.3 2.1 fusion.74
  210.6 3.0 convolution_convert_fusion
  213.6 35.4 %reduce-scatter.5.cloned.1.call-done = bf16[128,1536]{1,0:T(8,128)(2,1)} async-done(((bf16[512,1536]{1,0:T(8,128)(2,1)}), bf16[128,1536]{1,0:T(8,128)(2,1)}) %reduce-scatter.5.cloned.1.call-update) | async-done | bytes 393232 | tf_op jit(solution)/shard_map/reduce_scatter | solution.py:109
  249.1 1.8 convert_reduce_fusion
  251.3 30.4 %all_gather.19 = bf16[128,128]{1,0:T(8,128)(2,1)S(1)} all-gather(bf16[8,128]{1,0:T(8,128)(2,1)S(1)} %get-tuple-element.110), channel_id=1, replica_groups=mesh['groups'=2,'seq'=4,'pair'=4] {'seq','pair'}, dimensions={0}, use_global_device_ids=true | all-gather | bytes 34816 | tf_op jit(solution)/shard_map/all_gather | solution.py:125
  281.7 11.9 %all_gather.18 = bf16[32,128]{1,0:T(8,128)(2,1)S(1)} all-gather(bf16[8,128]{1,0:T(8,128)(2,1)S(1)} %get-tuple-element.109), channel_id=1, replica_groups=mesh['groups'=2,'seq'=4,'pair'=4] {'pair'}, dimensions={0}, use_global_device_ids=true | all-gather | bytes 10240 | tf_op jit(solution)/shard_map/all_gather | solution.py:124
  293.6 2.1 fusion.15
  (79 shorter events, 17.8 us)
Async XLA Ops:
  7.2 134.5 %copy-start = (bf16[1536,768]{1,0:T(8,128)(2,1)S(1)}, bf16[1536,768]{1,0:T(8,128)(2,1)}, u32[]{:S(2)}) copy-start(bf16[1536,768]{1,0:T(8,128)(2,1)} %param.16) | copy-start | bytes 7077892
  7.2 94.2 %reduce-scatter.3.cloned.1.call-start = ((), (), s32[]{:S(2)}) async-start(), calls=%async_computation.3 | async-start | bytes 3932160 | tf_op jit(solution)/shard_map/reduce_scatter | solution.py:52
  27.6 5.3 %copy-start.2 = (bf16[5,384,1536]{2,1,0:T(8,128)(2,1)S(1)}, bf16[5,384,1536]{2,1,0:T(8,128)(2,1)}, u32[]{:S(2)}) copy-start(bf16[5,384,1536]{2,1,0:T(8,128)(2,1)} %param.14) | copy-start | bytes 17694724
  27.6 5.3 %collective-permute-start = (bf16[8,384]{1,0:T(8,128)(2,1)S(1)}, bf16[8,384]{1,0:T(8,128)(2,1)S(1)}, u32[]{:S(2)}, u32[]{:S(2)}) collective-permute-start(bf16[8,384]{1,0:T(8,128)(2,1)S(1)} %get-tuple-element.107), channel_id=1, source_target_pairs={{0,4},{4,8},{8,12},{1,5},{5,9},{9,13},{2,6},{6,10},{10,14},{3,7},{... | collective-permute-start | bytes 18440 | tf_op jit(solution)/shard_map/ppermute | solution.py:22
  31.5 4.7 %collective-permute-start.1 = (bf16[8,384]{1,0:T(8,128)(2,1)S(1)}, bf16[8,384]{1,0:T(8,128)(2,1)S(1)}, u32[]{:S(2)}, u32[]{:S(2)}) collective-permute-start(bf16[8,384]{1,0:T(8,128)(2,1)S(1)} %get-tuple-element.108), channel_id=1, source_target_pairs={{4,0},{8,4},{12,8},{5,1},{9,5},{13,9},{6,2},{10,6},{14,10},{7,3},{... | collective-permute-start | bytes 18440 | tf_op jit(solution)/shard_map/ppermute | solution.py:23
  40.8 60.6 %copy-start.3 = (bf16[128,1536]{1,0:T(8,128)(2,1)S(1)}, bf16[128,1536]{1,0:T(8,128)(2,1)}, u32[]{:S(2)}) copy-start(bf16[128,1536]{1,0:T(8,128)(2,1)} %param.12) | copy-start | bytes 1179652
  40.8 62.7 %copy-start.7 = (f32[1536]{0:T(1024)S(1)}, f32[1536]{0:T(1024)}, u32[]{:S(2)}) copy-start(f32[1536]{0:T(1024)} %param.15) | copy-start | bytes 18436
  40.8 100.9 %all-gather.4.cloned.1.call-start = ((), (), s32[]{:S(2)}) async-start(), calls=%async_computation.4 | async-start | bytes 1966080 | tf_op jit(solution)/shard_map/all_gather | solution.py:61
  102.7 0.8 copy-start.4
  104.4 60.7 %all-gather.6.cloned.1.call-start = ((), (), s32[]{:S(2)}) async-start(), calls=%async_computation.5 | async-start | bytes 1310720 | tf_op jit(solution)/shard_map/all_gather | solution.py:77
  149.4 33.9 %all-gather.8.cloned.1.call-start = ((), (), s32[]{:S(2)}) async-start(), calls=%async_computation.6 | async-start | bytes 1310720 | tf_op jit(solution)/shard_map/all_gather | solution.py:78
  151.2 97.9 %reduce-scatter.5.cloned.1.call-start = ((), (), s32[]{:S(2)}) async-start(), calls=%async_computation.7 | async-start | bytes 1966080 | tf_op jit(solution)/shard_map/reduce_scatter | solution.py:109
  188.7 2.2 copy-start.1
  194.9 2.2 copy-start.1
  201.1 2.2 copy-start.1
  207.3 2.2 copy-start.1
  210.5 38.5 %copy-start.5 = (bf16[128,1536]{1,0:T(8,128)(2,1)S(1)}, bf16[128,1536]{1,0:T(8,128)(2,1)}, u32[]{:S(2)}) copy-start(bf16[128,1536]{1,0:T(8,128)(2,1)} %copy-done.4) | copy-start | bytes 1179652
  210.6 40.4 %copy-start.6 = (bf16[1536,256]{1,0:T(8,128)(2,1)S(1)}, bf16[1536,256]{1,0:T(8,128)(2,1)}, u32[]{:S(2)}) copy-start(bf16[1536,256]{1,0:T(8,128)(2,1)} %param.19) | copy-start | bytes 2359300
  210.6 40.4 %copy-start.8 = (f32[1536]{0:T(1024)S(1)}, f32[1536]{0:T(1024)}, u32[]{:S(2)}) copy-start(f32[1536]{0:T(1024)} %param.18) | copy-start | bytes 18436
Sparse Core Ops, SparseCore 0:
  40.9 60.4 reduce-scatter.2
  104.5 37.0 all-gather.3
  149.5 15.5 all-gather.5
  166.6 16.7 all-gather.7
  213.7 35.2 reduce-scatter.4
where the time goes:
time: 303 us; the launch traced here: 302 us
  waiting for transfers between devices  166 us (55%)
  blocking collectives  60 us (20%)
  matrix products  27.2 us (9%)
  local copies, waits for them, and re-layouts  17.1 us (6%)
  other arithmetic  15.3 us (5%)
  between operations  14 us (5%)
  starting transfers between devices  3.04 us (1%)
    reduce_scatter x1, waiting for transfers between devices, shards(): lax.psum_scatter(conv_rows(padded, conv_weight, row_count * lax.axis_size...  60.6 us
    all_gather x1, waiting for transfers between devices, shards(): lax.all_gather(attn_in, 'pair', axis=0, tiled=True)  37.2 us
    reduce_scatter x1, waiting for transfers between devices, shards(): lax.psum_scatter(jnp.dot(attended, w_out, preferred_element_type=jnp.floa...  35.4 us
    all_gather x1, blocking collectives, shards(): all_right = lax.all_gather(right_side, ('seq', 'pair'), axis=0, tiled=True)  30.4 us
    all_to_all x1, blocking collectives, shards(): lax.all_to_all(normed, 'pair', split_axis=1, concat_axis=0, tiled=True)  17.8 us
    all_gather x1, waiting for transfers between devices, shards(): value_piece = lax.all_gather(value_rows, 'seq', axis=0, tiled=True)  16 us
    all_gather x1, waiting for transfers between devices, shards(): key_piece = lax.all_gather(key_rows, 'seq', axis=0, tiled=True)  13.8 us
    all_gather x1, blocking collectives, shards(): row_side = lax.all_gather(left_side, 'pair', axis=0, tiled=True)  11.9 us
  transfers between devices with their start and end apart: 7, of which 6 were waited for; matrix products, arithmetic and copies ran while one was open for 2% of the time, Pallas kernels for 0%

commit v1 on v0

--- a/solution.py
+++ b/solution.py
@@ -74,8 +74,11 @@
         jnp.zeros((head_count, local_rows, VALUE_SIZE), jnp.float32),
     )
     carried = start_state
-    key_piece = lax.all_gather(key_rows, "seq", axis=0, tiled=True)
-    value_piece = lax.all_gather(value_rows, "seq", axis=0, tiled=True)
+    key_piece, value_piece = jnp.split(
+        lax.all_gather(jnp.concatenate([key_rows, value_rows], axis=1), "seq", axis=0, tiled=True),
+        [key_rows.shape[1]],
+        axis=1,
+    )
     piece_rows = key_piece.shape[0]
     block_rows = math.gcd(piece_rows, 512)
     block_count = piece_rows // block_rows

time: 303 us -> 295 us (0.974)
  waiting for transfers between devices: 166 us -> 157 us
    all_gather x2 -> x1, waiting for transfers between devices: 29.9 us -> 21.5 us  [shards(): lax.all_gather(jnp.concatenate([key_rows, value_rows], axis=1), 'seq', ax...]
  transfers between devices with their start and end apart: 7 -> 6, of which waited for: 6 -> 5; matrix products, arithmetic and copies ran while one was open for 2% -> 1% of each run, Pallas kernels for 0% -> 0%
where the time goes in v1:
time: 295 us
  waiting for transfers between devices  157 us (53%)
  blocking collectives  60 us (20%)
  matrix products  27.3 us (9%)
  local copies, waits for them, and re-layouts  17 us (6%)
  other arithmetic  16.2 us (5%)
  between operations  14 us (5%)
  starting transfers between devices  3 us (1%)
    reduce_scatter x1, waiting for transfers between devices, shards(): lax.psum_scatter(conv_rows(padded, conv_weight, row_count * lax.axis_size...  60.6 us
    all_gather x1, waiting for transfers between devices, shards(): lax.all_gather(attn_in, 'pair', axis=0, tiled=True)  37.2 us
    reduce_scatter x1, waiting for transfers between devices, shards(): lax.psum_scatter(jnp.dot(attended, w_out, preferred_element_type=jnp.floa...  35.4 us
    all_gather x1, blocking collectives, shards(): all_right = lax.all_gather(right_side, ('seq', 'pair'), axis=0, tiled=True)  30.4 us
    all_gather x1, waiting for transfers between devices, shards(): lax.all_gather(jnp.concatenate([key_rows, value_rows], axis=1), 'seq', ax...  21.5 us
    all_to_all x1, blocking collectives, shards(): lax.all_to_all(normed, 'pair', split_axis=1, concat_axis=0, tiled=True)  17.8 us
    all_gather x1, blocking collectives, shards(): row_side = lax.all_gather(left_side, 'pair', axis=0, tiled=True)  11.9 us
    reduce_sum x4, other arithmetic, one_block(): running_sum = running_sum * shrink + jnp.sum(weights, axis=-1)  8.4 us
  transfers between devices with their start and end apart: 6, of which 5 were waited for; matrix products, arithmetic and copies ran while one was open for 1% of the time, Pallas kernels for 0%

profile of v1, /device:TPU:0, one launch (start us, length us, event | category | flops | bytes accessed | tf_op | source)
XLA Modules:
  0.0 294.7 jit_solution(15376484793078136844)
XLA Ops:
  9.8 17.8 %all_to_all.19 = bf16[128,4,384]{2,0,1:T(8,128)(2,1)S(1)} all-to-all(bf16[128,4,384]{2,0,1:T(8,128)(2,1)S(1)} %bitcast.82), channel_id=1, replica_groups=mesh['groups'=2,'seq'=4,'pair'=4] {'pair'}, dimensions={1} | all-to-all | bytes 786432 | tf_op jit(solution)/shard_map/all_to_all | solution.py:50
  27.6 1.5 collective-permute-start
  29.1 2.4 fusion.19
  33.8 2.4 collective-permute-done.1
  38.1 2.6 fusion.10
  40.8 60.6 %reduce-scatter.3.cloned.1.call-done = f32[128,1536]{1,0:T(8,128)} async-done(((f32[512,1536]{1,0:T(8,128)}), f32[128,1536]{1,0:T(8,128)}) %reduce-scatter.3.cloned.1.call-update) | async-done | bytes 786448 | tf_op jit(solution)/shard_map/reduce_scatter | solution.py:52
  104.5 37.2 %all-gather.3.cloned.1.call-done = bf16[512,1536]{1,0:T(8,128)(2,1)} async-done(((bf16[128,1536]{1,0:T(8,128)(2,1)}), bf16[512,1536]{1,0:T(8,128)(2,1)}) %all-gather.3.cloned.1.call-update) | async-done | bytes 1572880 | tf_op jit(solution)/shard_map/all_gather | solution.py:61
  141.7 3.7 %convolution_convert_fusion.1 = bf16[512,768]{1,0:T(8,128)(2,1)} fusion(bf16[512,1536]{1,0:T(8,128)(2,1)} %all-gather.3.cloned.1.call-done, bf16[1536,768]{1,0:T(8,128)(2,1)S(1)} %copy-done), kind=kOutput, calls=%fused_computation.25 | convolution fusion | flops 1208352768 | bytes 4718592 | tf_op jit(solution)/shard_map/dot_general | solution.py:60
  145.4 2.1 reshape.71
  149.1 21.5 %all-gather.5.cloned.1.call-done = bf16[2048,512]{1,0:T(8,128)(2,1)} async-done(((bf16[512,512]{1,0:T(8,128)(2,1)}), bf16[2048,512]{1,0:T(8,128)(2,1)}) %all-gather.5.cloned.1.call-update) | async-done | bytes 2097168 | tf_op jit(solution)/shard_map/all_gather | solution.py:78
  170.6 3.0 %fusion.53 = (bf16[2048,256]{1,0:T(8,128)(2,1)}, bf16[2048,256]{1,0:T(8,128)(2,1)}) fusion(bf16[2048,512]{1,0:T(8,128)(2,1)} %all-gather.5.cloned.1.call-done), kind=kLoop, calls=%fused_computation.90 | loop fusion | bytes 4194304 | tf_op jit(solution)/shard_map/split | solution.py:77
  173.6 2.2 reshape.74
  175.7 2.1 reshape.75
  177.9 24.9 %while.15 = (s32[]{:T(128)}, f32[2,512]{1,0:T(2,128)S(1)}, f32[2,512]{1,0:T(2,128)S(1)}, f32[2,512,128]{2,1,0:T(8,128)S(1)}, bf16[4,512,2,128]{3,2,1,0:T(2,128)(...) while((s32[]{:T(128)}, f32[2,512]{1,0:T(2,128)S(1)}, ...), condition=%wide.region_6.7_spmd.clone, body=%wide.region_3.6_spmd.clone.sunk | while | flops 273028096 | bytes 17629320 | solution.py:108
  177.9 1.4 constant_dynamic-slice_fusion.3
  179.3 1.8 bitcast_reduce_fusion.2
  181.0 2.1 fusion.75
  184.1 1.4 constant_dynamic-slice_fusion.3
  185.5 1.8 bitcast_reduce_fusion.2
  187.3 2.1 fusion.75
  190.3 1.4 constant_dynamic-slice_fusion.3
  191.7 1.8 bitcast_reduce_fusion.2
  193.5 2.1 fusion.75
  196.5 1.4 constant_dynamic-slice_fusion.3
  197.9 1.8 bitcast_reduce_fusion.2
  199.7 2.1 fusion.75
  203.0 3.0 %convolution_convert_fusion = bf16[512,1536]{1,0:T(8,128)(2,1)} fusion(bf16[512,256]{0,1:T(8,128)(2,1)S(1)} %bitcast.84, bf16[256,1536]{1,0:T(8,128)(2,1)} %param.17), kind=kOutput, calls=%fused_computation.24 | convolution fusion | flops 403439616 | bytes 2621440 | tf_op jit(solution)/shard_map/dot_general | solution.py:113
  206.0 35.4 %reduce-scatter.5.cloned.1.call-done = bf16[128,1536]{1,0:T(8,128)(2,1)} async-done(((bf16[512,1536]{1,0:T(8,128)(2,1)}), bf16[128,1536]{1,0:T(8,128)(2,1)}) %reduce-scatter.5.cloned.1.call-update) | async-done | bytes 393232 | tf_op jit(solution)/shard_map/reduce_scatter | solution.py:112
  241.5 1.8 convert_reduce_fusion
  243.7 30.4 %all_gather.15 = bf16[128,128]{1,0:T(8,128)(2,1)S(1)} all-gather(bf16[8,128]{1,0:T(8,128)(2,1)S(1)} %get-tuple-element.112), channel_id=1, replica_groups=mesh['groups'=2,'seq'=4,'pair'=4] {'seq','pair'}, dimensions={0}, use_global_device_ids=true | all-gather | bytes 34816 | tf_op jit(solution)/shard_map/all_gather | solution.py:128
  274.1 11.9 %all_gather.14 = bf16[32,128]{1,0:T(8,128)(2,1)S(1)} all-gather(bf16[8,128]{1,0:T(8,128)(2,1)S(1)} %get-tuple-element.111), channel_id=1, replica_groups=mesh['groups'=2,'seq'=4,'pair'=4] {'pair'}, dimensions={0}, use_global_device_ids=true | all-gather | bytes 10240 | tf_op jit(solution)/shard_map/all_gather | solution.py:127
  286.0 2.1 fusion.15
  (77 shorter events, 15.9 us)
Async XLA Ops:
  7.2 134.6 %copy-start = (bf16[1536,768]{1,0:T(8,128)(2,1)S(1)}, bf16[1536,768]{1,0:T(8,128)(2,1)}, u32[]{:S(2)}) copy-start(bf16[1536,768]{1,0:T(8,128)(2,1)} %param.16) | copy-start | bytes 7077892
  7.2 94.2 %reduce-scatter.3.cloned.1.call-start = ((), (), s32[]{:S(2)}) async-start(), calls=%async_computation.3 | async-start | bytes 3932160 | tf_op jit(solution)/shard_map/reduce_scatter | solution.py:52
  27.6 5.3 %copy-start.2 = (bf16[5,384,1536]{2,1,0:T(8,128)(2,1)S(1)}, bf16[5,384,1536]{2,1,0:T(8,128)(2,1)}, u32[]{:S(2)}) copy-start(bf16[5,384,1536]{2,1,0:T(8,128)(2,1)} %param.14) | copy-start | bytes 17694724
  27.6 5.3 %collective-permute-start = (bf16[8,384]{1,0:T(8,128)(2,1)S(1)}, bf16[8,384]{1,0:T(8,128)(2,1)S(1)}, u32[]{:S(2)}, u32[]{:S(2)}) collective-permute-start(bf16[8,384]{1,0:T(8,128)(2,1)S(1)} %get-tuple-element.109), channel_id=1, source_target_pairs={{0,4},{4,8},{8,12},{1,5},{5,9},{9,13},{2,6},{6,10},{10,14},{3,7},{... | collective-permute-start | bytes 18440 | tf_op jit(solution)/shard_map/ppermute | solution.py:22
  31.5 4.7 %collective-permute-start.1 = (bf16[8,384]{1,0:T(8,128)(2,1)S(1)}, bf16[8,384]{1,0:T(8,128)(2,1)S(1)}, u32[]{:S(2)}, u32[]{:S(2)}) collective-permute-start(bf16[8,384]{1,0:T(8,128)(2,1)S(1)} %get-tuple-element.110), channel_id=1, source_target_pairs={{4,0},{8,4},{12,8},{5,1},{9,5},{13,9},{6,2},{10,6},{14,10},{7,3},{... | collective-permute-start | bytes 18440 | tf_op jit(solution)/shard_map/ppermute | solution.py:23
  40.8 60.6 %copy-start.3 = (bf16[128,1536]{1,0:T(8,128)(2,1)S(1)}, bf16[128,1536]{1,0:T(8,128)(2,1)}, u32[]{:S(2)}) copy-start(bf16[128,1536]{1,0:T(8,128)(2,1)} %param.12) | copy-start | bytes 1179652
  40.8 62.8 %copy-start.7 = (f32[1536]{0:T(1024)S(1)}, f32[1536]{0:T(1024)}, u32[]{:S(2)}) copy-start(f32[1536]{0:T(1024)} %param.15) | copy-start | bytes 18436
  40.8 100.9 %all-gather.3.cloned.1.call-start = ((), (), s32[]{:S(2)}) async-start(), calls=%async_computation.4 | async-start | bytes 1966080 | tf_op jit(solution)/shard_map/all_gather | solution.py:61
  102.7 0.8 copy-start.4
  104.5 66.1 %all-gather.5.cloned.1.call-start = ((), (), s32[]{:S(2)}) async-start(), calls=%async_computation.5 | async-start | bytes 2621440 | tf_op jit(solution)/shard_map/all_gather | solution.py:78
  149.0 92.5 %reduce-scatter.5.cloned.1.call-start = ((), (), s32[]{:S(2)}) async-start(), calls=%async_computation.6 | async-start | bytes 1966080 | tf_op jit(solution)/shard_map/reduce_scatter | solution.py:112
  181.0 2.2 copy-start.1
  187.3 2.2 copy-start.1
  193.5 2.2 copy-start.1
  199.7 2.2 copy-start.1
  203.0 38.5 %copy-start.5 = (bf16[128,1536]{1,0:T(8,128)(2,1)S(1)}, bf16[128,1536]{1,0:T(8,128)(2,1)}, u32[]{:S(2)}) copy-start(bf16[128,1536]{1,0:T(8,128)(2,1)} %copy-done.4) | copy-start | bytes 1179652
  203.0 40.5 %copy-start.6 = (bf16[1536,256]{1,0:T(8,128)(2,1)S(1)}, bf16[1536,256]{1,0:T(8,128)(2,1)}, u32[]{:S(2)}) copy-start(bf16[1536,256]{1,0:T(8,128)(2,1)} %param.19) | copy-start | bytes 2359300
  203.0 40.5 %copy-start.8 = (f32[1536]{0:T(1024)S(1)}, f32[1536]{0:T(1024)}, u32[]{:S(2)}) copy-start(f32[1536]{0:T(1024)} %param.18) | copy-start | bytes 18436
Sparse Core Ops, SparseCore 0:
  40.9 60.4 reduce-scatter.2
  104.6 37.1 all-gather.2
  149.1 21.4 all-gather.4
  206.2 35.2 reduce-scatter.4
